TPU v7x, 32 devices: a whole 2x2x4 slice. The times are simulated.
32 devices in a mesh: mol: 2 (over x), occ: 16 (over z, y, core).
Axes of the slice: x: 2, y: 2, z: 4, core: 2. Of those that a mesh axis runs over, the one named last changes fastest.
Arguments:
- integrals: bfloat16 [512, 128, 2048], P(('mol', 'occ')), parts along dimension 0, may hold values from -6 to 6
- orbitals: bfloat16 [4096, 1536], P('mol'), parts along dimension 0
- occ_energy: float32 [256], P('mol'), parts along dimension 0, may hold values from -2 to -0.3
- vir_energy: float32 [3072], P('mol'), parts along dimension 0, may hold values from 0.1 to 3
- owner: int32 [16], P('mol'), parts along dimension 0, may hold values from 0 to 127
- vblock: int32 [16], P('mol'), parts along dimension 0, may hold values from 0 to 7
Outputs:
- factors: bfloat16 [512, 128, 1536], P('mol', 'occ'), parts along dimension 0
- pair_energy: float32 [256, 8], P(('mol', 'occ')), parts along dimension 0
There are 2 independent parts, one for each index of `mol`. A program takes and returns all parts, laid end to end along the dimension named above; each array names one. Nothing has to cross between parts.
Inputs may be any that keep to these rules, and one draw needn't show every extreme that they name: `owner`: each step names one occupied orbital and one virtual block; steps may repeat.
All inputs are finite; a program needn't handle non-finite values.
Results may differ from a plain program's by a relative error of at most 0.001.
Values may be sent and summed in bfloat16 or wider, within the bound.
No kernel may reach another device: no remote copies, remote signals or barrier semaphores. Data moves between devices by JAX's collectives and lax.ppermute only.
A program may use at most 128 MiB of HBM per device.

v0:
```python
import jax
import jax.numpy as jnp
from jax import lax
from jax.sharding import PartitionSpec as P

VBLK = 192


def from_root(x, axis, root):
    mine = lax.axis_index(axis) == root
    return lax.psum(jnp.where(mine, x, jnp.zeros_like(x)), axis)


def pick_block(factors, orbital_j, block_id):
    local_count = factors.shape[1]
    row = orbital_j % local_count
    piece = lax.dynamic_slice(
        factors, (jnp.int32(0), row, block_id * VBLK), (factors.shape[0], 1, VBLK)
    )
    return (piece[:, 0, :], orbital_j // local_count)


def pair_column(factors, block, occ_here, occ_energy, vir_energy, orbital_j, block_id):
    coulomb = lax.dot_general(
        factors, block, (((0,), (0,)), ((), ())), preferred_element_type=jnp.float32
    )
    vir_block = lax.dynamic_slice(vir_energy, (block_id * VBLK,), (VBLK,))
    occ_j = occ_energy[orbital_j]
    denom = vir_energy[None, :, None] + vir_block[None, None, :] - occ_here[:, None, None] - occ_j
    scale = 1.0 / (factors.shape[0] * vir_energy.shape[0] * VBLK)
    return -jnp.sum(coulomb * coulomb / denom, axis=(1, 2)) * scale


def per_device(integrals, orbitals, occ_energy, vir_energy, owner, vblock):
    aux_here, occ_total, basis_count = integrals.shape
    step_count = owner.shape[0]
    flat = integrals.reshape(aux_here * occ_total, basis_count)
    product = jnp.dot(flat, orbitals, preferred_element_type=jnp.float32).astype(jnp.bfloat16)
    product = product.reshape(aux_here, occ_total, orbitals.shape[1])
    factors = lax.all_to_all(product, "occ", split_axis=1, concat_axis=0, tiled=True)
    local_count = factors.shape[1]
    occ_here = lax.dynamic_slice(occ_energy, (lax.axis_index("occ") * local_count,), (local_count,))
    energies = jnp.zeros((local_count, step_count), jnp.float32)

    def step_body(step, energies):
        orbital_j = owner[step]
        block_id = vblock[step]
        piece, root = pick_block(factors, orbital_j, block_id)
        block = from_root(piece, "occ", root)
        column = pair_column(factors, block, occ_here, occ_energy, vir_energy, orbital_j, block_id)
        return lax.dynamic_update_slice(energies, column[:, None], (jnp.int32(0), step))

    energies = lax.fori_loop(0, step_count, step_body, energies)
    return (factors, energies)


def solution(mesh):
    placed = (P(("mol", "occ"), None, None), P("mol", None), P("mol"), P("mol"), P("mol"), P("mol"))
    return jax.shard_map(
        per_device,
        mesh=mesh,
        in_specs=placed,
        out_specs=(P("mol", "occ", None), P(("mol", "occ"), None)),
        check_vma=False,
    )
```

profile of v0, /device:TPU:0, one launch (start us, length us, event | category | flops | bytes accessed | tf_op | source)
XLA Modules:
  0.0 991.6 jit_solution(14299061636335354797)
XLA Ops:
  7.2 17.3 %convolution_convert_fusion = bf16[2048,1536]{1,0:T(8,128)(2,1)S(1)} fusion(bf16[2048,2048]{1,0:T(8,128)(2,1)} %bitcast.42, bf16[2048,1536]{1,0:T(8,128)(2,1)} %param.9), kind=kOutput, calls=%fused_computation.6 | convolution fusion | flops 12888047616 | bytes 20971520 | tf_op jit(solution)/shard_map/dot_general | solution.py:38
  24.4 6.2 copy.13
  30.6 7.6 all-to-all-start
  38.3 114.1 %all-to-all-done = bf16[16,128,1536]{2,0,1:T(8,128)(2,1)} async-done(((bf16[16,128,1536]{2,0,1:T(8,128)(2,1)}), bf16[16,128,1536]{2,0,1:T(8,128)(2,1)}, u32[]{:S(2)}, u32[]{:S(2)}) %all-to-all-start) | async-done | bytes 6291488 | tf_op jit(solution)/shard_map/all_to_all | solution.py:40
  152.4 9.6 copy.14
  162.0 9.1 copy.15
  171.1 812.9 %while.15 = (s32[]{:T(128)}, f32[8,8]{0,1:T(8,128)S(1)}, s32[8]{0:T(128)S(1)}, s32[8]{0:T(128)S(1)}, bf16[256,8,1536]{0,2,1:T(8,128)(2,1)}, /*index=5*/f32[1536]...) while((s32[]{:T(128)}, f32[8,8]{0,1:T(8,128)S(1)}, ...), condition=%wide.region_3.4_spmd, body=%wide.region_0.3_spmd.sunk | while | flops 1220149248 | bytes 9544719 | solution.py:53
  175.6 1.6 select_bitcast_fusion.2
  179.3 108.6 %all-reduce.2.cloned.1.call-done = bf16[256,192]{0,1:T(8,128)(2,1)} async-done(((bf16[256,192]{0,1:T(8,128)(2,1)}), bf16[256,192]{0,1:T(8,128)(2,1)}) %all-reduce.2.cloned.1.call-update) | async-done | bytes 98320 | tf_op jit(solution)/shard_map/while/body/eval_jaxpr/psum | solution.py:11
  287.9 6.2 fusion.10
  298.6 1.6 select_bitcast_fusion.2
  302.3 84.2 %all-reduce.2.cloned.1.call-done = bf16[256,192]{0,1:T(8,128)(2,1)} async-done(((bf16[256,192]{0,1:T(8,128)(2,1)}), bf16[256,192]{0,1:T(8,128)(2,1)}) %all-reduce.2.cloned.1.call-update) | async-done | bytes 98320 | tf_op jit(solution)/shard_map/while/body/eval_jaxpr/psum | solution.py:11
  386.5 6.1 fusion.10
  397.2 1.6 select_bitcast_fusion.2
  400.9 84.2 %all-reduce.2.cloned.1.call-done = bf16[256,192]{0,1:T(8,128)(2,1)} async-done(((bf16[256,192]{0,1:T(8,128)(2,1)}), bf16[256,192]{0,1:T(8,128)(2,1)}) %all-reduce.2.cloned.1.call-update) | async-done | bytes 98320 | tf_op jit(solution)/shard_map/while/body/eval_jaxpr/psum | solution.py:11
  485.1 6.1 fusion.10
  495.7 1.6 select_bitcast_fusion.2
  499.5 84.2 %all-reduce.2.cloned.1.call-done = bf16[256,192]{0,1:T(8,128)(2,1)} async-done(((bf16[256,192]{0,1:T(8,128)(2,1)}), bf16[256,192]{0,1:T(8,128)(2,1)}) %all-reduce.2.cloned.1.call-update) | async-done | bytes 98320 | tf_op jit(solution)/shard_map/while/body/eval_jaxpr/psum | solution.py:11
  583.6 6.1 fusion.10
  594.3 1.6 select_bitcast_fusion.2
  598.0 84.2 %all-reduce.2.cloned.1.call-done = bf16[256,192]{0,1:T(8,128)(2,1)} async-done(((bf16[256,192]{0,1:T(8,128)(2,1)}), bf16[256,192]{0,1:T(8,128)(2,1)}) %all-reduce.2.cloned.1.call-update) | async-done | bytes 98320 | tf_op jit(solution)/shard_map/while/body/eval_jaxpr/psum | solution.py:11
  682.2 6.1 fusion.10
  692.9 1.6 select_bitcast_fusion.2
  696.6 84.2 %all-reduce.2.cloned.1.call-done = bf16[256,192]{0,1:T(8,128)(2,1)} async-done(((bf16[256,192]{0,1:T(8,128)(2,1)}), bf16[256,192]{0,1:T(8,128)(2,1)}) %all-reduce.2.cloned.1.call-update) | async-done | bytes 98320 | tf_op jit(solution)/shard_map/while/body/eval_jaxpr/psum | solution.py:11
  780.8 6.1 fusion.10
  791.4 1.6 select_bitcast_fusion.2
  795.1 84.2 %all-reduce.2.cloned.1.call-done = bf16[256,192]{0,1:T(8,128)(2,1)} async-done(((bf16[256,192]{0,1:T(8,128)(2,1)}), bf16[256,192]{0,1:T(8,128)(2,1)}) %all-reduce.2.cloned.1.call-update) | async-done | bytes 98320 | tf_op jit(solution)/shard_map/while/body/eval_jaxpr/psum | solution.py:11
  879.3 6.1 fusion.10
  890.0 1.6 select_bitcast_fusion.2
  893.7 84.2 %all-reduce.2.cloned.1.call-done = bf16[256,192]{0,1:T(8,128)(2,1)} async-done(((bf16[256,192]{0,1:T(8,128)(2,1)}), bf16[256,192]{0,1:T(8,128)(2,1)}) %all-reduce.2.cloned.1.call-update) | async-done | bytes 98320 | tf_op jit(solution)/shard_map/while/body/eval_jaxpr/psum | solution.py:11
  977.9 6.1 fusion.10
  984.1 0.7 copy.16
  (82 shorter events, 17.7 us)
Async XLA Ops:
  30.6 7.6 copy-start.3
  30.6 121.8 %all-to-all-start = ((bf16[16,128,1536]{2,0,1:T(8,128)(2,1)}), bf16[16,128,1536]{2,0,1:T(8,128)(2,1)}, u32[]{:S(2)}, u32[]{:S(2)}) async-start(bf16[16,128,1536]{2,0,1:T(8,128)(2,1)} %copy.13), calls=%async_computation | async-start | bytes 12582912 | tf_op jit(solution)/shard_map/all_to_all | solution.py:40
  162.0 9.1 copy-start
  162.0 9.1 copy-start.1
  162.0 9.1 copy-start.2
  171.2 116.8 %all-reduce.2.cloned.1.call-start = ((), (), s32[]{:S(2)}) async-start(), calls=%async_computation.1 | async-start | bytes 196608 | tf_op jit(solution)/shard_map/while/body/eval_jaxpr/psum | solution.py:11
  294.1 92.4 %all-reduce.2.cloned.1.call-start = ((), (), s32[]{:S(2)}) async-start(), calls=%async_computation.1 | async-start | bytes 196608 | tf_op jit(solution)/shard_map/while/body/eval_jaxpr/psum | solution.py:11
  392.7 92.4 %all-reduce.2.cloned.1.call-start = ((), (), s32[]{:S(2)}) async-start(), calls=%async_computation.1 | async-start | bytes 196608 | tf_op jit(solution)/shard_map/while/body/eval_jaxpr/psum | solution.py:11
  491.3 92.4 %all-reduce.2.cloned.1.call-start = ((), (), s32[]{:S(2)}) async-start(), calls=%async_computation.1 | async-start | bytes 196608 | tf_op jit(solution)/shard_map/while/body/eval_jaxpr/psum | solution.py:11
  589.8 92.4 %all-reduce.2.cloned.1.call-start = ((), (), s32[]{:S(2)}) async-start(), calls=%async_computation.1 | async-start | bytes 196608 | tf_op jit(solution)/shard_map/while/body/eval_jaxpr/psum | solution.py:11
  688.4 92.4 %all-reduce.2.cloned.1.call-start = ((), (), s32[]{:S(2)}) async-start(), calls=%async_computation.1 | async-start | bytes 196608 | tf_op jit(solution)/shard_map/while/body/eval_jaxpr/psum | solution.py:11
  787.0 92.4 %all-reduce.2.cloned.1.call-start = ((), (), s32[]{:S(2)}) async-start(), calls=%async_computation.1 | async-start | bytes 196608 | tf_op jit(solution)/shard_map/while/body/eval_jaxpr/psum | solution.py:11
  885.5 92.4 %all-reduce.2.cloned.1.call-start = ((), (), s32[]{:S(2)}) async-start(), calls=%async_computation.1 | async-start | bytes 196608 | tf_op jit(solution)/shard_map/while/body/eval_jaxpr/psum | solution.py:11
Sparse Core Ops, SparseCore 0:
  177.3 110.5 all-reduce.1
  300.3 86.1 all-reduce.1
  398.9 86.1 all-reduce.1
  497.5 86.1 all-reduce.1
  596.0 86.1 all-reduce.1
  694.6 86.1 all-reduce.1
  793.1 86.1 all-reduce.1
  891.7 86.1 all-reduce.1
where the time goes:
time: 993 us; the launch traced here: 992 us
  waiting for transfers between devices  812 us (82%)
  matrix products  66.4 us (7%)
  local copies, waits for them, and re-layouts  41.6 us (4%)
  loops' own time  35.7 us (4%)
  between operations  14.1 us (1%)
  other arithmetic  13.8 us (1%)
    psum x8, waiting for transfers between devices, from_root(): return lax.psum(jnp.where(mine, x, jnp.zeros_like(x)), axis)  698 us
    all_to_all x1, waiting for transfers between devices, per_device(): lax.all_to_all(product, 'occ', split_axis=1, concat_axis=0, tiled=True)  114 us
    dot_general x8, matrix products, pair_column(): lax.dot_general(factors, block, (((0,), (0,)), ((), ())), preferred_eleme...  49.2 us
    another operation x1, loops' own time, per_device(): energies = lax.fori_loop(0, step_count, step_body, energies)  35.7 us
  transfers between devices with their start and end apart: 9, of which 9 were waited for; matrix products, arithmetic and copies ran while one was open for 1% of the time, Pallas kernels for 0%

commit v1 on v0

--- a/solution.py
+++ b/solution.py
@@ -37,7 +37,10 @@
     flat = integrals.reshape(aux_here * occ_total, basis_count)
     product = jnp.dot(flat, orbitals, preferred_element_type=jnp.float32).astype(jnp.bfloat16)
     product = product.reshape(aux_here, occ_total, orbitals.shape[1])
-    factors = lax.all_to_all(product, "occ", split_axis=1, concat_axis=0, tiled=True)
+    factors = jnp.concatenate(
+        lax.all_to_all(jnp.stack(jnp.split(product, lax.axis_size("occ"), axis=1)), "occ", 0, 0),
+        axis=0,
+    )
     local_count = factors.shape[1]
     occ_here = lax.dynamic_slice(occ_energy, (lax.axis_index("occ") * local_count,), (local_count,))
     energies = jnp.zeros((local_count, step_count), jnp.float32)

time: 993 us -> 995 us (level)
    unnamed x9 -> x25, local copies, waits for them, and re-layouts: 0.68 us -> 18.2 us
where the time goes in v1:
time: 995 us; the launch traced here: 994 us
  waiting for transfers between devices  812 us (82%)
  matrix products  66.4 us (7%)
  local copies, waits for them, and re-layouts  44.1 us (4%)
  loops' own time  35.7 us (4%)
  between operations  14.1 us (1%)
  other arithmetic  13.8 us (1%)
    psum x8, waiting for transfers between devices, from_root(): return lax.psum(jnp.where(mine, x, jnp.zeros_like(x)), axis)  698 us
    all_to_all x1, waiting for transfers between devices, per_device(): lax.all_to_all(jnp.stack(jnp.split(product, lax.axis_size('occ'), axis=1)...  114 us
    dot_general x8, matrix products, pair_column(): lax.dot_general(factors, block, (((0,), (0,)), ((), ())), preferred_eleme...  49.2 us
    another operation x1, loops' own time, per_device(): energies = lax.fori_loop(0, step_count, step_body, energies)  35.7 us
  transfers between devices with their start and end apart: 9, of which 9 were waited for; matrix products, arithmetic and copies ran while one was open for 1% of the time, Pallas kernels for 0%

profile of v1, /device:TPU:0, one launch (start us, length us, event | category | flops | bytes accessed | tf_op | source)
XLA Modules:
  0.0 994.1 jit_solution(7420790037926338550)
XLA Ops:
  7.2 17.3 %convolution_convert_fusion = bf16[2048,1536]{1,0:T(8,128)(2,1)S(1)} fusion(bf16[2048,2048]{1,0:T(8,128)(2,1)} %bitcast.116, bf16[2048,1536]{1,0:T(8,128)(2,1)} %param.9), kind=kOutput, calls=%fused_computation.6 | convolution fusion | flops 12888047616 | bytes 20971520 | tf_op jit(solution)/shard_map/dot_general | solution.py:38
  26.0 0.8 fusion.15
  28.3 0.8 fusion.12
  36.8 7.6 all-to-all-start
  44.5 114.1 %all-to-all-done = bf16[16,16,8,1536]{3,2,1,0:T(8,128)(2,1)} async-done(((bf16[16,16,8,1536]{3,2,1,0:T(8,128)(2,1)}), bf16[16,16,8,1536]{3,2,1,0:T(8,128)(2,1)}, u32[]{:S(2)}, u32[]{:S(2)}) %all-to-all-start) | async-done | bytes 6291488 | tf_op jit(solution)/shard_map/all_to_all | solution.py:41
  158.6 9.1 copy.9
  167.7 813.0 %while.15 = (s32[]{:T(128)}, f32[8,8]{0,1:T(8,128)S(1)}, s32[8]{0:T(128)S(1)}, s32[8]{0:T(128)S(1)}, bf16[256,8,1536]{0,2,1:T(8,128)(2,1)}, /*index=5*/f32[1536]...) while((s32[]{:T(128)}, f32[8,8]{0,1:T(8,128)S(1)}, ...), condition=%wide.region_3.4_spmd, body=%wide.region_0.3_spmd.sunk | while | flops 1220149248 | bytes 9544719 | solution.py:56
  172.2 1.6 select_bitcast_fusion.2
  175.9 108.6 %all-reduce.2.cloned.1.call-done = bf16[256,192]{0,1:T(8,128)(2,1)} async-done(((bf16[256,192]{0,1:T(8,128)(2,1)}), bf16[256,192]{0,1:T(8,128)(2,1)}) %all-reduce.2.cloned.1.call-update) | async-done | bytes 98320 | tf_op jit(solution)/shard_map/while/body/eval_jaxpr/psum | solution.py:11
  284.5 6.1 fusion.26
  295.1 1.6 select_bitcast_fusion.2
  298.8 84.2 %all-reduce.2.cloned.1.call-done = bf16[256,192]{0,1:T(8,128)(2,1)} async-done(((bf16[256,192]{0,1:T(8,128)(2,1)}), bf16[256,192]{0,1:T(8,128)(2,1)}) %all-reduce.2.cloned.1.call-update) | async-done | bytes 98320 | tf_op jit(solution)/shard_map/while/body/eval_jaxpr/psum | solution.py:11
  383.0 6.1 fusion.26
  393.7 1.6 select_bitcast_fusion.2
  397.4 84.2 %all-reduce.2.cloned.1.call-done = bf16[256,192]{0,1:T(8,128)(2,1)} async-done(((bf16[256,192]{0,1:T(8,128)(2,1)}), bf16[256,192]{0,1:T(8,128)(2,1)}) %all-reduce.2.cloned.1.call-update) | async-done | bytes 98320 | tf_op jit(solution)/shard_map/while/body/eval_jaxpr/psum | solution.py:11
  481.6 6.1 fusion.26
  492.3 1.6 select_bitcast_fusion.2
  496.0 84.2 %all-reduce.2.cloned.1.call-done = bf16[256,192]{0,1:T(8,128)(2,1)} async-done(((bf16[256,192]{0,1:T(8,128)(2,1)}), bf16[256,192]{0,1:T(8,128)(2,1)}) %all-reduce.2.cloned.1.call-update) | async-done | bytes 98320 | tf_op jit(solution)/shard_map/while/body/eval_jaxpr/psum | solution.py:11
  580.2 6.1 fusion.26
  590.9 1.6 select_bitcast_fusion.2
  594.6 84.2 %all-reduce.2.cloned.1.call-done = bf16[256,192]{0,1:T(8,128)(2,1)} async-done(((bf16[256,192]{0,1:T(8,128)(2,1)}), bf16[256,192]{0,1:T(8,128)(2,1)}) %all-reduce.2.cloned.1.call-update) | async-done | bytes 98320 | tf_op jit(solution)/shard_map/while/body/eval_jaxpr/psum | solution.py:11
  678.8 6.1 fusion.26
  689.5 1.6 select_bitcast_fusion.2
  693.2 84.2 %all-reduce.2.cloned.1.call-done = bf16[256,192]{0,1:T(8,128)(2,1)} async-done(((bf16[256,192]{0,1:T(8,128)(2,1)}), bf16[256,192]{0,1:T(8,128)(2,1)}) %all-reduce.2.cloned.1.call-update) | async-done | bytes 98320 | tf_op jit(solution)/shard_map/while/body/eval_jaxpr/psum | solution.py:11
  777.4 6.1 fusion.26
  788.0 1.6 select_bitcast_fusion.2
  791.8 84.2 %all-reduce.2.cloned.1.call-done = bf16[256,192]{0,1:T(8,128)(2,1)} async-done(((bf16[256,192]{0,1:T(8,128)(2,1)}), bf16[256,192]{0,1:T(8,128)(2,1)}) %all-reduce.2.cloned.1.call-update) | async-done | bytes 98320 | tf_op jit(solution)/shard_map/while/body/eval_jaxpr/psum | solution.py:11
  876.0 6.1 fusion.26
  886.6 1.6 select_bitcast_fusion.2
  890.3 84.2 %all-reduce.2.cloned.1.call-done = bf16[256,192]{0,1:T(8,128)(2,1)} async-done(((bf16[256,192]{0,1:T(8,128)(2,1)}), bf16[256,192]{0,1:T(8,128)(2,1)}) %all-reduce.2.cloned.1.call-update) | async-done | bytes 98320 | tf_op jit(solution)/shard_map/while/body/eval_jaxpr/psum | solution.py:11
  974.6 6.1 fusion.26
  981.4 5.9 copy.36
  (97 shorter events, 29.2 us)
Async XLA Ops:
  36.8 7.6 copy-start.3
  36.8 121.8 %all-to-all-start = ((bf16[16,16,8,1536]{3,2,1,0:T(8,128)(2,1)}), bf16[16,16,8,1536]{3,2,1,0:T(8,128)(2,1)}, u32[]{:S(2)}, u32[]{:S(2)}) async-start(bf16[16,16,8,1536]{3,2,1,0:T(8,128)(2,1)} %fusion.2), calls=%async_computation | async-start | bytes 12582912 | tf_op jit(solution)/shard_map/all_to_all | solution.py:41
  158.6 9.1 copy-start
  158.6 9.1 copy-start.1
  158.6 9.1 copy-start.2
  167.7 116.8 %all-reduce.2.cloned.1.call-start = ((), (), s32[]{:S(2)}) async-start(), calls=%async_computation.1 | async-start | bytes 196608 | tf_op jit(solution)/shard_map/while/body/eval_jaxpr/psum | solution.py:11
  290.6 92.4 %all-reduce.2.cloned.1.call-start = ((), (), s32[]{:S(2)}) async-start(), calls=%async_computation.1 | async-start | bytes 196608 | tf_op jit(solution)/shard_map/while/body/eval_jaxpr/psum | solution.py:11
  389.2 92.4 %all-reduce.2.cloned.1.call-start = ((), (), s32[]{:S(2)}) async-start(), calls=%async_computation.1 | async-start | bytes 196608 | tf_op jit(solution)/shard_map/while/body/eval_jaxpr/psum | solution.py:11
  487.8 92.4 %all-reduce.2.cloned.1.call-start = ((), (), s32[]{:S(2)}) async-start(), calls=%async_computation.1 | async-start | bytes 196608 | tf_op jit(solution)/shard_map/while/body/eval_jaxpr/psum | solution.py:11
  586.4 92.4 %all-reduce.2.cloned.1.call-start = ((), (), s32[]{:S(2)}) async-start(), calls=%async_computation.1 | async-start | bytes 196608 | tf_op jit(solution)/shard_map/while/body/eval_jaxpr/psum | solution.py:11
  685.0 92.4 %all-reduce.2.cloned.1.call-start = ((), (), s32[]{:S(2)}) async-start(), calls=%async_computation.1 | async-start | bytes 196608 | tf_op jit(solution)/shard_map/while/body/eval_jaxpr/psum | solution.py:11
  783.6 92.4 %all-reduce.2.cloned.1.call-start = ((), (), s32[]{:S(2)}) async-start(), calls=%async_computation.1 | async-start | bytes 196608 | tf_op jit(solution)/shard_map/while/body/eval_jaxpr/psum | solution.py:11
  882.2 92.4 %all-reduce.2.cloned.1.call-start = ((), (), s32[]{:S(2)}) async-start(), calls=%async_computation.1 | async-start | bytes 196608 | tf_op jit(solution)/shard_map/while/body/eval_jaxpr/psum | solution.py:11
Sparse Core Ops, SparseCore 0:
  173.9 110.5 all-reduce.1
  296.8 86.1 all-reduce.1
  395.4 86.1 all-reduce.1
  494.0 86.1 all-reduce.1
  592.6 86.1 all-reduce.1
  691.2 86.1 all-reduce.1
  789.8 86.1 all-reduce.1
  888.3 86.1 all-reduce.1
